TPU v7x, 256 devices: a whole 4x4x8 slice. The times are simulated.
256 devices in a mesh: row: 8 (over y, core), col: 32 (over x, z).
Axes of the slice: x: 4, y: 4, z: 8, core: 2. Of those that a mesh axis runs over, the one named last changes fastest.
Arguments:
- trailing_adjoint: float32 [12288, 12288], P('row', 'col'), may hold values from -3 to 3, as said below
- panel: float32 [12288, 256], P(('row', 'col')), may hold values from -0.0546875 to 0.0546875
- panel_adjoint: float32 [12288, 256], P(('row', 'col')), may hold values from -6 to 6
- diag_factor: float32 [256, 256], replicated, may hold values from -1 to 2, as said below
- diag_adjoint: float32 [256, 256], P('row', 'col'), may hold values from -6 to 6
Outputs:
- off_adjoint: float32 [12288, 256], P(('row', 'col'))
- block_adjoint: float32 [256, 256], replicated
Inputs may be any that keep to these rules, and one draw needn't show every extreme that they name: `trailing_adjoint`: symmetric. `diag_factor`: lower triangular with diagonal entries from 1 to 2.
All inputs are finite; a program needn't handle non-finite values.
Results may differ from a plain program's by a relative error of at most 0.000071.
Values sent between devices are 32-bit elements; how exact they have to be, the bound alone decides.
No kernel may reach another device: no remote copies, remote signals or barrier semaphores. Data moves between devices by JAX's collectives and lax.ppermute only.
A program may use at most 64 MiB of HBM per device.

v0:
```python
import jax
import jax.numpy as jnp
from jax import lax
from jax.sharding import PartitionSpec as P


def right_solve(factor, rows):
    return jax.scipy.linalg.solve_triangular(factor, rows.T, lower=True, trans=1).T


def left_solve(factor, matrix):
    return jax.scipy.linalg.solve_triangular(factor, matrix, lower=True, trans=1)


def diagonal_adjoint(factor, adjoint):
    product = jnp.dot(
        factor.T, adjoint, precision=lax.Precision.HIGHEST, preferred_element_type=jnp.float32
    )
    lower = jnp.tril(product) - 0.5 * jnp.diag(jnp.diag(product))
    symmetric = lower + lower.T
    half = left_solve(factor, symmetric)
    return 0.5 * left_solve(factor, half.T).T


def body(trailing_adjoint, panel, panel_adjoint, diag_factor, diag_adjoint):
    nrows = lax.axis_size("row")
    stretch = panel.shape[0]
    span = stretch * nrows
    col_index = lax.axis_index("col")
    gathered = lax.all_gather(panel, ("row", "col"), axis=0, tiled=True)
    column_rows = lax.dynamic_slice_in_dim(gathered, col_index * span, span, 0)
    product = lax.psum_scatter(
        jnp.dot(
            trailing_adjoint,
            column_rows,
            precision=lax.Precision.HIGHEST,
            preferred_element_type=jnp.float32,
        ),
        "col",
        scatter_dimension=0,
        tiled=True,
    )
    updated = panel_adjoint - 2.0 * product
    off_adjoint = right_solve(diag_factor, updated)
    local_term = jnp.dot(
        off_adjoint.T, panel, precision=lax.Precision.HIGHEST, preferred_element_type=jnp.float32
    )
    row_piece = lax.all_gather(diag_adjoint, "col", axis=1, tiled=True)
    full_adjoint = lax.all_gather(row_piece, "row", axis=0, tiled=True)
    total = lax.psum(local_term, ("row", "col"))
    accumulated = full_adjoint - total
    return (off_adjoint, diagonal_adjoint(diag_factor, accumulated))


def solution(mesh):
    return jax.shard_map(
        body,
        mesh=mesh,
        in_specs=(
            P("row", "col"),
            P(("row", "col"), None),
            P(("row", "col"), None),
            P(),
            P("row", "col"),
        ),
        out_specs=(P(("row", "col"), None), P()),
        check_vma=False,
    )
```

profile of v0, /device:TPU:2, one launch (start us, length us, event | category | flops | bytes accessed | tf_op | source)
XLA Modules:
  0.0 632.7 jit_solution(16761037603501634626)
XLA Ops:
  7.2 0.7 all-gather.2.cloned.1.call-update
  8.0 127.5 %all-gather.2.cloned.1.call-done = f32[12288,256]{1,0:T(8,128)} async-done(((f32[48,256]{1,0:T(8,128)}), f32[12288,256]{1,0:T(8,128)}) %all-gather.2.cloned.1.call-update) | async-done | bytes 12582928 | tf_op jit(solution)/shard_map/all_gather | solution.py:30
  135.4 6.2 convolution_bitcast_fusion
  141.6 3.1 copy.24
  144.8 41.9 %all_gather.10 = f32[32,256]{0,1:T(8,128)S(1)} all-gather(f32[32,8]{0,1:T(8,128)S(1)} %copy-done.4), channel_id=1, replica_groups=mesh['row'=8,'col'=32] {'col'}, dimensions={1}, use_global_device_ids=true | all-gather | bytes 33792 | tf_op jit(solution)/shard_map/all_gather | solution.py:48
  186.9 4.1 while.5
  186.9 0.6 fusion.32
  187.5 1.4 bitcast_dynamic-update-slice_fusion.2
  188.9 0.6 fusion.32
  189.5 1.4 bitcast_dynamic-update-slice_fusion.2
  191.0 19.7 %custom-call.7 = f32[2,128,128]{1,2,0:T(8,128)S(1)} custom-call(f32[2,128,128]{2,1,0:T(8,128)S(1)} %get-tuple-element.18), custom_call_target="InvertDiagBlocksLowerTriangular" | custom-call | tf_op jit(solution)/shard_map/jit(_solve_triangular)/triangular_solve | solution.py:8
  210.7 12.8 %all_gather.11 = f32[256,256]{1,0:T(8,128)S(1)} all-gather(f32[32,256]{1,0:T(8,128)S(1)} %copy.19), channel_id=1, replica_groups=mesh['row'=8,'col'=32] {'row'}, dimensions={0}, use_global_device_ids=true | all-gather | bytes 294912 | tf_op jit(solution)/shard_map/all_gather | solution.py:49
  223.5 136.2 %reduce-scatter.4.cloned.1.call-done = f32[48,256]{1,0:T(8,128)} async-done(((f32[1536,256]{1,0:T(8,128)}), f32[48,256]{1,0:T(8,128)}) %reduce-scatter.4.cloned.1.call-update) | async-done | bytes 49168 | tf_op jit(solution)/shard_map/reduce_scatter | solution.py:32
  359.7 0.8 subtract_bitcast_fusion
  361.2 1.1 fusion.16
  362.4 0.6 fusion.17
  363.0 256.3 %all-reduce.2.cloned.1.call-done = f32[256,256]{1,0:T(8,128)} async-done(((f32[256,256]{1,0:T(8,128)}), f32[256,256]{1,0:T(8,128)}) %all-reduce.2.cloned.1.call-update) | async-done | bytes 262160 | tf_op jit(solution)/shard_map/psum | solution.py:50
  619.3 1.6 fusion.2
  621.0 2.3 gather_fusion
  623.7 0.3 convolution_subtract_fusion.1
  624.4 0.3 fusion.5
  624.6 0.4 convolution_subtract_fusion
  625.0 0.3 fusion.10
  625.3 0.8 copy.22
  (32 shorter events, 1.8 us)
Async XLA Ops:
  7.2 128.3 %copy-start = (f32[1536,384]{1,0:T(8,128)S(1)}, f32[1536,384]{1,0:T(8,128)}, u32[]{:S(2)}) copy-start(f32[1536,384]{1,0:T(8,128)} %param.7) | copy-start | bytes 7077892
  7.2 128.2 %all-gather.2.cloned.1.call-start = ((), (), s32[]{:S(2)}) async-start(), calls=%async_computation.1 | async-start | bytes 12632064 | tf_op jit(solution)/shard_map/all_gather | solution.py:30
  7.9 351.8 %reduce-scatter.4.cloned.1.call-start = ((), (), s32[]{:S(2)}) async-start(), calls=%async_computation.3 | async-start | bytes 1622016 | tf_op jit(solution)/shard_map/reduce_scatter | solution.py:32
  141.6 3.2 copy-start.4
  141.6 45.1 %copy-start.1 = (f32[256,256]{1,0:T(8,128)S(1)}, f32[256,256]{1,0:T(8,128)}, u32[]{:S(2)}) copy-start(f32[256,256]{1,0:T(8,128)} %param.10) | copy-start | bytes 786436
  144.7 215.1 %copy-start.3 = (f32[48,256]{1,0:T(8,128)S(1)}, f32[48,256]{1,0:T(8,128)}, u32[]{:S(2)}) copy-start(f32[48,256]{1,0:T(8,128)} %param.9) | copy-start | bytes 147460
  144.7 216.5 %copy-start.2 = (f32[48,256]{1,0:T(8,128)S(1)}, f32[48,256]{1,0:T(8,128)}, u32[]{:S(2)}) copy-start(f32[48,256]{1,0:T(8,128)} %param.8) | copy-start | bytes 147460
  144.7 474.6 %all-reduce.2.cloned.1.call-start = ((), (), s32[]{:S(2)}) async-start(), calls=%async_computation.2 | async-start | bytes 524288 | tf_op jit(solution)/shard_map/psum | solution.py:50
Sparse Core Ops, SparseCore 0:
  11.8 123.5 all-gather.1
  144.8 214.8 reduce-scatter.3
  365.8 253.4 all-reduce.1
where the time goes:
time: 633 us
  waiting for transfers between devices  521 us (82%)
  blocking collectives  54.7 us (9%)
  other arithmetic  21.3 us (3%)
  between operations  13.9 us (2%)
  matrix products  11.2 us (2%)
  local copies, waits for them, and re-layouts  10.6 us (2%)
    psum x1, waiting for transfers between devices, body(): total = lax.psum(local_term, ('row', 'col'))  256 us
    reduce_scatter x1, waiting for transfers between devices, body(): lax.psum_scatter(jnp.dot(trailing_adjoint, column_rows, precision=lax.Pre...  136 us
    all_gather x1, waiting for transfers between devices, body(): gathered = lax.all_gather(panel, ('row', 'col'), axis=0, tiled=True)  127 us
    all_gather x1, blocking collectives, body(): row_piece = lax.all_gather(diag_adjoint, 'col', axis=1, tiled=True)  41.9 us
    another operation x3, other arithmetic, right_solve(): jax.scipy.linalg.solve_triangular(factor, rows.T, lower=True, trans=1)  19.7 us
    all_gather x1, blocking collectives, body(): full_adjoint = lax.all_gather(row_piece, 'row', axis=0, tiled=True)  12.8 us
  transfers between devices with their start and end apart: 3, of which 3 were waited for; matrix products, arithmetic and copies ran while one was open for 4% of the time, Pallas kernels for 0%

commit v1 on v0

--- a/solution.py
+++ b/solution.py
@@ -27,7 +27,10 @@
     stretch = panel.shape[0]
     span = stretch * nrows
     col_index = lax.axis_index("col")
-    gathered = lax.all_gather(panel, ("row", "col"), axis=0, tiled=True)
+    gathered = jnp.concatenate(
+        lax.all_to_all(jnp.stack([panel] * lax.axis_size(("row", "col"))), ("row", "col"), 0, 0),
+        axis=0,
+    )
     column_rows = lax.dynamic_slice_in_dim(gathered, col_index * span, span, 0)
     product = lax.psum_scatter(
         jnp.dot(

time: 633 us -> 802 us (1.27)
  waiting for transfers between devices: 521 us -> 667 us
  starting transfers between devices: 0.12 us -> 15.6 us
    all_to_all x0 -> x1, waiting for transfers between devices: none -> 275 us  [body(): lax.all_to_all(jnp.stack([panel] * lax.axis_size(('row', 'col'))), ('row'...]
    all_gather x1 -> x0, waiting for transfers between devices: 127 us -> none  [body(): gathered = lax.all_gather(panel, ('row', 'col'), axis=0, tiled=True)]
    all_to_all x0 -> x1, starting transfers between devices: none -> 15.6 us  [body(): lax.all_to_all(jnp.stack([panel] * lax.axis_size(('row', 'col'))), ('row'...]
  transfers between devices with their start and end apart: 3 -> 3, of which waited for: 3 -> 3; matrix products, arithmetic and copies ran while one was open for 4% -> 3% of each run, Pallas kernels for 0% -> 0%
where the time goes in v1:
time: 802 us
  waiting for transfers between devices  667 us (83%)
  blocking collectives  54.8 us (7%)
  other arithmetic  21.3 us (3%)
  local copies, waits for them, and re-layouts  17.5 us (2%)
  starting transfers between devices  15.6 us (2%)
  between operations  14.2 us (2%)
  matrix products  11.3 us (1%)
    all_to_all x1, waiting for transfers between devices, body(): lax.all_to_all(jnp.stack([panel] * lax.axis_size(('row', 'col'))), ('row'...  275 us
    psum x1, waiting for transfers between devices, body(): total = lax.psum(local_term, ('row', 'col'))  256 us
    reduce_scatter x1, waiting for transfers between devices, body(): lax.psum_scatter(jnp.dot(trailing_adjoint, column_rows, precision=lax.Pre...  136 us
    all_gather x1, blocking collectives, body(): row_piece = lax.all_gather(diag_adjoint, 'col', axis=1, tiled=True)  41.8 us
    another operation x3, other arithmetic, right_solve(): jax.scipy.linalg.solve_triangular(factor, rows.T, lower=True, trans=1)  19.7 us
  transfers between devices with their start and end apart: 3, of which 3 were waited for; matrix products, arithmetic and copies ran while one was open for 3% of the time, Pallas kernels for 0%

profile of v1, /device:TPU:2, one launch (start us, length us, event | category | flops | bytes accessed | tf_op | source)
XLA Modules:
  0.0 801.6 jit_solution(3201606763346870750)
XLA Ops:
  7.2 7.0 stack.2
  14.2 15.6 %all-to-all-start = ((f32[256,48,256]{2,1,0:T(8,128)}), f32[256,48,256]{2,1,0:T(8,128)}, u32[]{:S(2)}, u32[]{:S(2)}) async-start(f32[256,48,256]{2,1,0:T(8,128)} %stack.2), calls=%async_computation | async-start | bytes 25165824 | tf_op jit(solution)/shard_map/all_to_all | solution.py:31
  29.8 274.8 %all-to-all-done = f32[256,48,256]{2,1,0:T(8,128)} async-done(((f32[256,48,256]{2,1,0:T(8,128)}), f32[256,48,256]{2,1,0:T(8,128)}, u32[]{:S(2)}, u32[]{:S(2)}) %all-to-all-start) | async-done | bytes 12582944 | tf_op jit(solution)/shard_map/all_to_all | solution.py:31
  304.6 6.2 convolution_bitcast_fusion
  310.8 3.1 copy.24
  314.1 4.0 while.5
  314.1 0.6 fusion.32
  314.7 1.4 bitcast_dynamic-update-slice_fusion.2
  316.1 0.6 fusion.32
  316.7 1.4 bitcast_dynamic-update-slice_fusion.2
  318.0 19.7 %custom-call.7 = f32[2,128,128]{1,2,0:T(8,128)S(1)} custom-call(f32[2,128,128]{2,1,0:T(8,128)S(1)} %get-tuple-element.18), custom_call_target="InvertDiagBlocksLowerTriangular" | custom-call | tf_op jit(solution)/shard_map/jit(_solve_triangular)/triangular_solve | solution.py:8
  337.7 41.8 %all_gather.6 = f32[32,256]{0,1:T(8,128)S(1)} all-gather(f32[32,8]{0,1:T(8,128)S(1)} %copy-done.3), channel_id=1, replica_groups=mesh['row'=8,'col'=32] {'col'}, dimensions={1}, use_global_device_ids=true | all-gather | bytes 33792 | tf_op jit(solution)/shard_map/all_gather | solution.py:51
  379.6 13.0 %all_gather.7 = f32[256,256]{1,0:T(8,128)S(1)} all-gather(f32[32,256]{1,0:T(8,128)S(1)} %copy.19), channel_id=1, replica_groups=mesh['row'=8,'col'=32] {'row'}, dimensions={0}, use_global_device_ids=true | all-gather | bytes 294912 | tf_op jit(solution)/shard_map/all_gather | solution.py:52
  392.6 135.9 %reduce-scatter.4.cloned.1.call-done = f32[48,256]{1,0:T(8,128)} async-done(((f32[1536,256]{1,0:T(8,128)}), f32[48,256]{1,0:T(8,128)}) %reduce-scatter.4.cloned.1.call-update) | async-done | bytes 49168 | tf_op jit(solution)/shard_map/reduce_scatter | solution.py:35
  528.5 0.8 subtract_bitcast_fusion
  530.0 1.1 fusion.16
  531.2 0.6 fusion.17
  531.8 256.1 %all-reduce.2.cloned.1.call-done = f32[256,256]{1,0:T(8,128)} async-done(((f32[256,256]{1,0:T(8,128)}), f32[256,256]{1,0:T(8,128)}) %all-reduce.2.cloned.1.call-update) | async-done | bytes 262160 | tf_op jit(solution)/shard_map/psum | solution.py:53
  787.9 1.6 fusion.2
  789.6 2.3 gather_fusion
  792.3 0.3 convolution_subtract_fusion.1
  793.0 0.3 fusion.5
  793.3 0.4 convolution_subtract_fusion
  794.0 0.8 copy.22
  (30 shorter events, 2.0 us)
Async XLA Ops:
  7.2 297.5 %copy-start = (f32[1536,384]{1,0:T(8,128)S(1)}, f32[1536,384]{1,0:T(8,128)}, u32[]{:S(2)}) copy-start(f32[1536,384]{1,0:T(8,128)} %param.7) | copy-start | bytes 7077892
  14.2 290.4 %all-to-all-start = ((f32[256,48,256]{2,1,0:T(8,128)}), f32[256,48,256]{2,1,0:T(8,128)}, u32[]{:S(2)}, u32[]{:S(2)}) async-start(f32[256,48,256]{2,1,0:T(8,128)} %stack.2), calls=%async_computation | async-start | bytes 25165824 | tf_op jit(solution)/shard_map/all_to_all | solution.py:31
  29.8 498.7 %reduce-scatter.4.cloned.1.call-start = ((), (), s32[]{:S(2)}) async-start(), calls=%async_computation.3 | async-start | bytes 1622016 | tf_op jit(solution)/shard_map/reduce_scatter | solution.py:35
  310.8 3.2 copy-start.1
  310.8 26.9 %copy-start.3 = (f32[32,8]{0,1:T(8,128)S(1)}, f32[32,8]{0,1:T(8,128)}, u32[]{:S(2)}) copy-start(f32[32,8]{0,1:T(8,128)} %param.11) | copy-start | bytes 3076
  313.9 216.1 %copy-start.2 = (f32[48,256]{1,0:T(8,128)S(1)}, f32[48,256]{1,0:T(8,128)}, u32[]{:S(2)}) copy-start(f32[48,256]{1,0:T(8,128)} %param.8) | copy-start | bytes 147460
  313.9 474.0 %all-reduce.2.cloned.1.call-start = ((), (), s32[]{:S(2)}) async-start(), calls=%async_computation.2 | async-start | bytes 524288 | tf_op jit(solution)/shard_map/psum | solution.py:53
Sparse Core Ops, SparseCore 0:
  314.0 214.4 reduce-scatter.3
  534.5 253.3 all-reduce.1
